TPU v7x, 32 devices: a whole 2x2x4 slice. The times are simulated.
32 devices in a mesh: groups: 2 (over y), lat: 4 (over x, core), lon: 4 (over z).
Axes of the slice: x: 2, y: 2, z: 4, core: 2. Of those that a mesh axis runs over, the one named last changes fastest.
Arguments:
- tracers: float32 [256, 256, 128], P(('groups', 'lat'), 'lon'), parts along dimension 0, may hold values from 0.3 to 12.6, as said below
- shifts: float32 [4, 3, 16, 32], P('groups'), parts along dimension 0, may hold values from 0 to 1
- diffusivity: float32 [128], P('lat'), may hold values from 0.02 to 0.2, as said below
- source_patch: int32 [4, 16, 32], P('groups'), parts along dimension 0, may hold values from 0 to 511, as said below
Outputs:
- advanced: float32 [256, 256, 128], P(('groups', 'lat'), 'lon'), parts along dimension 0
There are 2 independent parts, one for each index of `groups`. A program takes and returns all parts, laid end to end along the dimension named above; an argument that names none is the same for every part. Nothing has to cross between parts.
Inputs may be any that keep to these rules, and one draw needn't show every extreme that they name: `source_patch`: entry [s, r, c] is the global index of the departure patch of destination patch (r, c) in step s; the departure patch lies in the same tile of 8 patch columns as the destination, and in the same band of 4 patch rows or in one of the two bands on either side. For each step, tile, destination band and other source band, at most 4 destination patches take their departure patch there, and every destination band has a source band that gives exactly 4. `tracers`: positive mixing ratios. `diffusivity`: positive diffusion numbers.
All inputs are finite; a program needn't handle non-finite values.
Results may differ from a plain program's by a relative error of at most 0.0003.
Values sent between devices are 32-bit elements; how exact they have to be, the bound alone decides.
No kernel may reach another device: no remote copies, remote signals or barrier semaphores. Data moves between devices by JAX's collectives and lax.ppermute only.
A program may use at most 64 MiB of HBM per device.

v0:
```python
import math
import jax
import jax.numpy as jnp
from jax import lax
from jax.sharding import PartitionSpec as P

LEV = 4
STEPS = 2
CAP = 4


def from_behind(block, axis, distance):
    devices = range(lax.axis_size(axis))
    route = [(i - distance, i) for i in devices if i - distance in devices]
    return lax.ppermute(block, axis, route)


def extended(cells, sides, width, closed):
    for axis, dim in sides:
        count = lax.axis_size(axis)
        ends = count if closed else count - 1
        head = lax.slice_in_dim(cells, 0, width, axis=dim)
        tail = lax.slice_in_dim(cells, cells.shape[dim] - width, cells.shape[dim], axis=dim)
        cells = jnp.concatenate(
            [
                lax.ppermute(tail, axis, [(i, (i + 1) % count) for i in range(ends)]),
                cells,
                lax.ppermute(head, axis, [((i + 1) % count, i) for i in range(ends)]),
            ],
            axis=dim,
        )
    return cells


def cubic_weights(fraction):
    first_term = -fraction * (fraction - 1.0) * (fraction - 2.0) / 6.0
    second_term = (fraction + 1.0) * (fraction - 1.0) * (fraction - 2.0) / 2.0
    third_term = -(fraction + 1.0) * fraction * (fraction - 2.0) / 2.0
    fourth_term = (fraction + 1.0) * fraction * (fraction - 1.0) / 6.0
    return (first_term, second_term, third_term, fourth_term)


def cubic_matrix(fraction, extent):
    places = jnp.arange(extent)
    running = jnp.zeros(fraction.shape + (extent, extent), jnp.float32)
    for offset, weight in zip(range(-1, 3), cubic_weights(fraction)):
        target_col = jnp.clip(places + offset, 0, extent - 1)
        indicator = (target_col[:, None] == places[None, :]).astype(jnp.float32)
        running = running + weight[..., None, None] * indicator
    return running


def interpolate(patches, fraction_y, fraction_x, fraction_z):
    patch_count = patches.shape[0]
    value_count = patches.shape[2]
    weight_y = cubic_matrix(fraction_y, 8)
    weight_x = cubic_matrix(fraction_x, 8)
    plane_weights = jnp.einsum(
        "nac,nbd->nabcd", weight_y, weight_x, precision=lax.Precision.HIGHEST
    ).reshape(patch_count, 64, 64)
    flat_result = jnp.einsum(
        "nij,njv->niv", plane_weights, patches, precision=lax.Precision.HIGHEST
    )
    stacked = flat_result.reshape(patch_count, 64, LEV, value_count // LEV)
    weight_z = cubic_matrix(fraction_z, LEV)
    levelled = jnp.einsum("nlm,nimt->nilt", weight_z, stacked, precision=lax.Precision.HIGHEST)
    return levelled.reshape(patch_count, 64, value_count)


def to_patches(state_field):
    band_rows = state_field.shape[0] // 8
    band_cols = state_field.shape[1] // 8
    return (
        state_field.reshape(band_rows, 8, band_cols, 8, -1)
        .transpose(0, 2, 1, 3, 4)
        .reshape(band_rows * band_cols, 64, -1)
    )


def from_patches(patches, band_rows, band_cols):
    return (
        patches.reshape(band_rows, band_cols, 8, 8, -1)
        .transpose(0, 2, 1, 3, 4)
        .reshape(band_rows * 8, band_cols * 8, -1)
    )


def column_area(first_row, row_count, total_rows):
    latitude = ((first_row + jnp.arange(row_count)).astype(jnp.float32) + 0.5) * (
        math.pi / total_rows
    ) - 0.5 * math.pi
    return jnp.cos(latitude)


def column_mass(state_field, weights):
    return jnp.sum(weights[:, None, None] * state_field, axis=(0, 1))


def local(tracers, shifts, diffusivity, source_patch):
    lat_count = lax.axis_size("lat")
    lat_index = lax.axis_index("lat")
    lon_index = lax.axis_index("lon")
    row_count, col_count, value_count = tracers.shape
    band_rows = row_count // 8
    band_cols = col_count // 8
    per_device = band_rows * band_cols
    total_cols = source_patch.shape[2]
    band_offsets = (-2, -1, 1, 2)
    weights = column_area(lat_index * row_count, row_count, row_count * lat_count)
    devices = jnp.arange(lat_count)
    slot_range = jnp.arange(CAP)
    state_field = tracers
    target = lax.psum(column_mass(tracers, weights), ("lat", "lon"))
    for step_index in range(STEPS):
        column_ids = lax.dynamic_slice_in_dim(
            source_patch[step_index], lon_index * band_cols, band_cols, 1
        ).reshape(lat_count, per_device)
        fractions = lax.dynamic_slice_in_dim(
            shifts[step_index], lon_index * band_cols, band_cols, 2
        ).reshape(3, lat_count, per_device)
        source_row = column_ids // total_cols
        source_dev = source_row // band_rows
        source_local = (
            source_row % band_rows * band_cols + column_ids % total_cols - lon_index * band_cols
        )
        remote = source_dev != devices[:, None]
        matches = (source_dev[:, :, None] == devices[None, None, :]) & remote[:, :, None]
        slot_ranks = jnp.cumsum(matches.astype(jnp.int32), axis=1) - 1
        slot_of = jnp.sum(jnp.where(matches, slot_ranks, 0), axis=2)
        owned_here = remote & (source_dev == lat_index)
        sending = owned_here[:, :, None] & (slot_of[:, :, None] == slot_range[None, None, :])
        send_local = jnp.sum(jnp.where(sending, source_local[:, :, None], 0), axis=1)
        near_local = jnp.stack(
            [
                lax.dynamic_index_in_dim(send_local, lat_index + offset, 0, keepdims=False)
                for offset in band_offsets
            ]
        )
        own_patches = to_patches(state_field)
        send_patches = own_patches[near_local.reshape(-1)]
        my_dev = lax.dynamic_index_in_dim(source_dev, lat_index, 0, keepdims=False)
        my_slot = lax.dynamic_index_in_dim(slot_of, lat_index, 0, keepdims=False)
        my_local = lax.dynamic_index_in_dim(source_local, lat_index, 0, keepdims=False)
        my_remote = lax.dynamic_index_in_dim(remote, lat_index, 0, keepdims=False)
        my_frac = lax.dynamic_index_in_dim(fractions, lat_index, 1, keepdims=False)
        my_offset = lat_index - my_dev
        pick_index = jnp.where(my_offset < 0, my_offset + 2, my_offset + 1) * CAP + my_slot
        send_frac = jnp.sum(jnp.where(sending[None], fractions[:, :, :, None], 0.0), axis=2)
        near_frac = jnp.stack(
            [
                lax.dynamic_index_in_dim(send_frac, lat_index + offset, 1, keepdims=False)
                for offset in band_offsets
            ],
            axis=1,
        ).reshape(3, -1)
        outgoing = interpolate(send_patches, near_frac[0], near_frac[1], near_frac[2])
        outgoing = outgoing.reshape(4, CAP, 64, value_count)
        arrived = jnp.stack(
            [
                from_behind(outgoing[slot_place], "lat", offset)
                for slot_place, offset in enumerate(band_offsets)
            ]
        )
        arrived = arrived.reshape(4 * CAP, 64, value_count)
        local_done = interpolate(own_patches[my_local], my_frac[0], my_frac[1], my_frac[2])
        finished = jnp.where(my_remote[:, None, None], arrived[pick_index], local_done)
        advected = from_patches(finished, band_rows, band_cols)
        lon_wide = extended(advected, (("lon", 1),), 1, True)
        lat_wide = extended(advected, (("lat", 0),), 1, False)
        laplace = lat_wide[2:] + lat_wide[:-2] + lon_wide[:, 2:] + lon_wide[:, :-2] - 4.0 * advected
        diffused = advected + diffusivity[:, None, None] * laplace
        step_total = lax.psum(column_mass(diffused, weights), ("lat", "lon"))
        state_field = diffused * (target / step_total)[None, None, :]
    return state_field


def solution(mesh):
    return jax.shard_map(
        local,
        mesh=mesh,
        in_specs=(
            P(("groups", "lat"), "lon", None),
            P("groups", None, None, None),
            P("lat"),
            P("groups", None, None),
        ),
        out_specs=P(("groups", "lat"), "lon", None),
        check_vma=False,
    )
```

profile of v0, /device:TPU:0, one launch (start us, length us, event | category | flops | bytes accessed | tf_op | source)
XLA Modules:
  0.0 196.2 jit_solution(16985384277161938453)
XLA Ops:
  0.0 0.8 fusion.146
  2.4 1.4 copy.61
  7.5 1.5 copy.62
  9.6 2.9 %fusion.150 = f32[16,64,128]{1,2,0:T(8,128)S(1)} fusion(f32[16,64,64]{2,1,0:T(8,128)} %copy.62, f32[16,64,128]{2,1,0:T(8,128)S(1)} %gather_fusion), kind=kOutput, calls=%fused_computation.360 | convolution fusion | flops 100663296 | bytes 1310720 | tf_op jit(solution)/shard_map/nij,njv->niv/dot_general | solution.py:61
  12.5 2.5 %convolution_bitcast_fusion.1 = f32[16,64,4,32]{1,2,3,0:T(4,128)S(1)} fusion(f32[16,64,4,32]{1,3,2,0:T(8,128)S(1)} %bitcast.153, f32[4,4]{1,0:T(4,128)S(1)} %fusion.111, f32[16]{0:T(128)S(1)} %get-tuple-element.115, f32[4,4]{1,0:T(4,128)S(1)} %fusion.110, f32[16]{0:T(128)S(1)} %get-tuple-element.116, f32[4,4]{1,0:T(4,128)S(1)} %fusion.109, ...), kind=kOutput, calls=%fused_computation.13 | convolution fusion | flops 6293248 | bytes 1049088 | tf_op jit(solution)/shard_map/nlm,nimt->nilt/dot_general | solution.py:66
  15.2 1.3 collective-permute-start
  17.2 1.3 collective-permute-start.1
  19.2 3.7 %collective-permute-start.2 = (f32[4,64,128]{1,2,0:T(8,128)}, f32[4,64,128]{1,2,0:T(8,128)}, u32[]{:S(2)}, u32[]{:S(2)}) collective-permute-start(f32[4,64,128]{1,2,0:T(8,128)} %bitcast.16), channel_id=1, source_target_pairs={{0,4},{4,8},{8,12},{1,5},{5,9},{9,13},{2,6},{6,10},{10,14},{3,7},{... | collective-permute-start | bytes 393224 | tf_op jit(solution)/shard_map/ppermute | solution.py:15
  23.7 6.3 %collective-permute-start.3 = (f32[4,64,128]{1,2,0:T(8,128)}, f32[4,64,128]{1,2,0:T(8,128)}, u32[]{:S(2)}, u32[]{:S(2)}) collective-permute-start(f32[4,64,128]{1,2,0:T(8,128)} %bitcast.18), channel_id=1, source_target_pairs={{0,8},{4,12},{1,9},{5,13},{2,10},{6,14},{3,11},{7,15},{16,24},{20,... | collective-permute-start | bytes 393224 | tf_op jit(solution)/shard_map/ppermute | solution.py:15
  34.1 1.7 copy.70
  35.8 0.8 pad_clamp_fusion.3
  37.9 1.2 pad_clamp_fusion
  39.1 1.1 multiply_multiply_fusion.2
  41.7 3.5 %fusion.151 = f32[32,64,128]{1,2,0:T(8,128)S(1)} fusion(f32[32,64,64]{2,1,0:T(8,128)S(1)} %copy-done.1, f32[32,64,128]{2,1,0:T(8,128)S(1)} %gather_fusion.2), kind=kOutput, calls=%fused_computation.361 | convolution fusion | flops 201326592 | bytes 2621440 | tf_op jit(solution)/shard_map/nij,njv->niv/dot_general | solution.py:61
  45.2 1.6 broadcast_multiply_fusion
  47.1 5.6 %fusion.4 = f32[32,64,4,32]{1,2,3,0:T(4,128)} fusion(f32[32,64,4,32]{1,3,2,0:T(8,128)S(1)} %bitcast.143, f32[4,4]{1,0:T(4,128)S(1)} %copy-done.10, f32[32]{0:T(128)S(1)} %get-tuple-element.105, f32[4,4]{1,0:T(4,128)S(1)} %copy-done.8, f32[32]{0:T(128)S(1)} %get-tuple-element.106, f32[4,4]{1,0:T(4,128)S(1)} %copy-done.6, f32[32]{0:T(128)S(1)} %get-tuple-element.104, ...), kind=kOutput, calls=%fused_computation.10 | convolution fusion | flops 12586496 | bytes 2097920 | tf_op jit(solution)/shard_map/nlm,nimt->nilt/dot_general | solution.py:66
  53.4 4.8 %copy.73 = f32[32,64,4,32]{3,2,1,0:T(4,128)} copy(f32[32,64,4,32]{1,2,3,0:T(4,128)} %fusion.4) | data formatting | bytes 2097152 | tf_op jit(solution)/shard_map/nlm,nimt->nilt/transpose | solution.py:66
  58.2 4.5 %reshape.1437 = f32[4,8,8,8,128]{4,3,2,1,0:T(8,128)} reshape(f32[32,64,4,32]{3,2,1,0:T(4,128)} %copy.73) | data formatting | bytes 2097152 | tf_op jit(solution)/shard_map/reshape | solution.py:67
  62.9 2.3 %pad_maximum_fusion.8 = f32[4,4,64,128]{2,3,1,0:T(8,128)} fusion(f32[1,4,64,128]{2,3,1,0:T(8,128)} %bitcast.19, f32[1,4,64,128]{2,3,1,0:T(8,128)} %bitcast.17, f32[1,4,64,128]{2,3,1,0:T(8,128)} %bitcast.15, f32[1,4,64,128]{2,3,1,0:T(8,128)} %bitcast.13), kind=kLoop, calls=%fused_computation.34 | loop fusion | flops 393216 | bytes 1048576 | tf_op jit(solution)/shard_map/stack | solution.py:158
  65.2 1.5 copy.69
  66.7 1.6 gather_fusion.1
  68.3 1.7 select_bitcast_fusion.1
  70.2 1.3 collective-permute-start.4
  71.5 3.0 %collective-permute-start.5 = (f32[1,64,128]{2,1,0:T(8,128)S(1)}, f32[1,64,128]{2,1,0:T(8,128)S(1)}, u32[]{:S(2)}, u32[]{:S(2)}) collective-permute-start(f32[1,64,128]{2,1,0:T(8,128)S(1)} %get-tuple-element.36), channel_id=1, source_target_pairs={{0,4},{4,8},{8,12},{1,5},{5,9},{9,13},{2,6},{6,10},{10,14},{3,7},{... | collective-permute-start | bytes 98312 | tf_op jit(solution)/shard_map/ppermute | solution.py:26
  74.5 4.8 %collective-permute-start.6 = (f32[32,1,128]{2,1,0:T(1,128)S(1)}, f32[32,1,128]{2,1,0:T(1,128)S(1)}, u32[]{:S(2)}, u32[]{:S(2)}) collective-permute-start(f32[32,1,128]{2,1,0:T(1,128)S(1)} %get-tuple-element.37), channel_id=1, source_target_pairs={{1,0},{2,1},{3,2},{0,3},{5,4},{6,5},{7,6},{4,7},{9,8},{10,9},{11,1... | collective-permute-start | bytes 49160 | tf_op jit(solution)/shard_map/ppermute | solution.py:28
  79.4 3.3 %copy.84 = f32[32,64,64]{2,1,0:T(8,128)} copy(f32[32,64,64]{0,2,1:T(8,128)} %bitcast.142) | data formatting | bytes 1048576 | tf_op jit(solution)/shard_map/reshape | solution.py:60
  82.7 1.4 copy.76
  84.9 1.9 multiply_reduce_fusion.1
  86.8 30.4 %all-reduce = (f32[128]{0:T(128)S(1)}, f32[128]{0:T(128)S(1)}) all-reduce(f32[128]{0:T(128)S(1)} %get-tuple-element.6, f32[128]{0:T(128)S(1)} %get-tuple-element.5), channel_id=1, replica_groups=mesh['groups'=2,'lat'=4,'lon'=4] {'lat','lon'}, use_global_device_ids=true, to_apply=%region_8.9 | all-reduce | flops 256 | bytes 2048 | tf_op jit(solution)/shard_map/psum | solution.py:113
  117.8 0.9 gather_fusion.5
  119.4 1.8 fusion.152
  121.3 2.5 %convolution_bitcast_fusion = f32[16,64,4,32]{1,2,3,0:T(4,128)S(1)} fusion(f32[16,64,4,32]{1,3,2,0:T(8,128)S(1)} %bitcast.154, f32[16]{0:T(128)S(1)} %copy-done.24, f32[16]{0:T(128)S(1)} %copy-done.25, f32[16]{0:T(128)S(1)} %copy-done.23, f32[16]{0:T(128)S(1)} %copy-done.22, f32[4,4]{1,0:T(4,128)S(1)} %copy-done.10, f32[4,4]{1,0:T(4,128)S(1)} %copy-done.8, ...), kind=kOutput, calls=%fused_computation.12 | convolution fusion | flops 6293248 | bytes 1049088 | tf_op jit(solution)/shard_map/nlm,nimt->nilt/dot_general | solution.py:66
  123.9 1.4 collective-permute-start.8
  125.4 1.3 collective-permute-start.9
  126.7 3.7 %collective-permute-start.10 = (f32[4,64,128]{1,2,0:T(8,128)S(1)}, f32[4,64,128]{1,2,0:T(8,128)}, u32[]{:S(2)}, u32[]{:S(2)}) collective-permute-start(f32[4,64,128]{1,2,0:T(8,128)S(1)} %bitcast.161), channel_id=1, source_target_pairs={{0,4},{4,8},{8,12},{1,5},{5,9},{9,13},{2,6},{6,10},{10,14},{3,7},{... | collective-permute-start | bytes 393224 | tf_op jit(solution)/shard_map/ppermute | solution.py:15
  130.5 6.3 %collective-permute-start.11 = (f32[4,64,128]{1,2,0:T(8,128)S(1)}, f32[4,64,128]{1,2,0:T(8,128)}, u32[]{:S(2)}, u32[]{:S(2)}) collective-permute-start(f32[4,64,128]{1,2,0:T(8,128)S(1)} %bitcast.162), channel_id=1, source_target_pairs={{0,8},{4,12},{1,9},{5,13},{2,10},{6,14},{3,11},{7,15},{16,24},{20,... | collective-permute-start | bytes 393224 | tf_op jit(solution)/shard_map/ppermute | solution.py:15
  136.8 3.5 %fusion.153 = f32[32,64,128]{1,2,0:T(8,128)S(1)} fusion(f32[32,64,64]{2,1,0:T(8,128)S(1)} %copy-done, f32[32,64,128]{2,1,0:T(8,128)S(1)} %gather_fusion.5), kind=kOutput, calls=%fused_computation.363 | convolution fusion | flops 201326592 | bytes 2621440 | tf_op jit(solution)/shard_map/nij,njv->niv/dot_general | solution.py:61
  140.3 4.5 %fusion.7 = f32[32,64,4,32]{1,2,3,0:T(4,128)S(1)} fusion(f32[32,64,4,32]{1,3,2,0:T(8,128)S(1)} %bitcast.144, f32[32]{0:T(128)S(1)} %copy-done.30, f32[32]{0:T(128)S(1)} %copy-done.31, f32[32]{0:T(128)S(1)} %copy-done.29, f32[32]{0:T(128)S(1)} %copy-done.27, f32[4,4]{1,0:T(4,128)S(1)} %copy-done.10, f32[4,4]{1,0:T(4,128)S(1)} %copy-done.8, ...), kind=kOutput, calls=%fused_computation.11 | convolution fusion | flops 12586496 | bytes 2097920 | tf_op jit(solution)/shard_map/nlm,nimt->nilt/dot_general | solution.py:66
  144.8 3.2 %copy.87 = f32[32,64,4,32]{3,2,1,0:T(4,128)} copy(f32[32,64,4,32]{1,2,3,0:T(4,128)S(1)} %fusion.7) | data formatting | bytes 2097152 | tf_op jit(solution)/shard_map/nlm,nimt->nilt/transpose | solution.py:66
  148.0 3.7 %reshape.1446 = f32[4,8,8,8,128]{4,3,2,1,0:T(8,128)S(1)} reshape(f32[32,64,4,32]{3,2,1,0:T(4,128)} %copy.87) | data formatting | bytes 2097152 | tf_op jit(solution)/shard_map/reshape | solution.py:67
  151.8 1.2 pad_maximum_fusion.9
  154.2 1.3 collective-permute-start.12
  155.5 3.0 %collective-permute-start.13 = (f32[1,64,128]{2,1,0:T(8,128)S(1)}, f32[1,64,128]{2,1,0:T(8,128)S(1)}, u32[]{:S(2)}, u32[]{:S(2)}) collective-permute-start(f32[1,64,128]{2,1,0:T(8,128)S(1)} %get-tuple-element.28), channel_id=1, source_target_pairs={{0,4},{4,8},{8,12},{1,5},{5,9},{9,13},{2,6},{6,10},{10,14},{3,7},{... | collective-permute-start | bytes 98312 | tf_op jit(solution)/shard_map/ppermute | solution.py:26
  158.7 2.0 %collective-permute-start.15 = (f32[32,1,128]{2,1,0:T(1,128)S(1)}, f32[32,1,128]{2,1,0:T(1,128)S(1)}, u32[]{:S(2)}, u32[]{:S(2)}) collective-permute-start(f32[32,1,128]{2,1,0:T(1,128)S(1)} %get-tuple-element.30), channel_id=1, source_target_pairs={{0,1},{1,2},{2,3},{3,0},{4,5},{5,6},{6,7},{7,4},{8,9},{9,10},{10,1... | collective-permute-start | bytes 49160 | tf_op jit(solution)/shard_map/ppermute | solution.py:26
  160.7 1.7 collective-permute-done.14
  162.4 1.9 collective-permute-done.15
  165.0 29.8 %psum.23 = f32[128]{0:T(128)S(1)} all-reduce(f32[128]{0:T(128)S(1)} %multiply_reduce_fusion), channel_id=1, replica_groups=mesh['groups'=2,'lat'=4,'lon'=4] {'lat','lon'}, use_global_device_ids=true, to_apply=%region_13.14 | all-reduce | flops 128 | bytes 1024 | tf_op jit(solution)/shard_map/psum | solution.py:172
  194.8 1.4 broadcast_multiply_fusion.4
  (196 shorter events, 20.4 us)
Async XLA Ops:
  3.8 8.7 %copy-start.3 = (f32[4,4]{1,0:T(4,128)}, f32[4,4]{1,0:T(4,128)S(1)}, u32[]{:S(2)}) copy-start(f32[4,4]{1,0:T(4,128)S(1)} %fusion.108) | copy-start | bytes 196
  3.9 8.6 %copy-start.5 = (f32[4,4]{1,0:T(4,128)}, f32[4,4]{1,0:T(4,128)S(1)}, u32[]{:S(2)}) copy-start(f32[4,4]{1,0:T(4,128)S(1)} %fusion.109) | copy-start | bytes 196
  3.9 8.6 %copy-start.7 = (f32[4,4]{1,0:T(4,128)}, f32[4,4]{1,0:T(4,128)S(1)}, u32[]{:S(2)}) copy-start(f32[4,4]{1,0:T(4,128)S(1)} %fusion.110) | copy-start | bytes 196
  4.0 8.5 %copy-start.9 = (f32[4,4]{1,0:T(4,128)}, f32[4,4]{1,0:T(4,128)S(1)}, u32[]{:S(2)}) copy-start(f32[4,4]{1,0:T(4,128)S(1)} %fusion.111) | copy-start | bytes 196
  4.1 0.6 copy-start.18
  4.1 1.3 copy-start.16
  4.1 1.4 copy-start.12
  4.1 4.8 %copy-start.20 = (pred[4,32]{1,0:T(4,128)(4,1)}, pred[4,32]{1,0:T(4,128)(4,1)S(1)}, u32[]{:S(2)}) copy-start(pred[4,32]{1,0:T(4,128)(4,1)S(1)} %get-tuple-element.129) | copy-start | bytes 388
  5.4 27.5 %copy-start.11 = (s32[4,32]{1,0:T(4,128)}, s32[4,32]{1,0:T(4,128)S(1)}, u32[]{:S(2)}) copy-start(s32[4,32]{1,0:T(4,128)S(1)} %select_reduce_fusion.3) | copy-start | bytes 1540
  15.0 17.8 %copy-start.21 = (pred[4,32]{1,0:T(4,128)(4,1)S(1)}, pred[4,32]{1,0:T(4,128)(4,1)}, u32[]{:S(2)}) copy-start(pred[4,32]{1,0:T(4,128)(4,1)} %copy-done.20) | copy-start | bytes 388
  15.2 47.7 %collective-permute-start = (f32[4,64,128]{1,2,0:T(8,128)S(1)}, f32[4,64,128]{1,2,0:T(8,128)}, u32[]{:S(2)}, u32[]{:S(2)}) collective-permute-start(f32[4,64,128]{1,2,0:T(8,128)S(1)} %bitcast.158), channel_id=1, source_target_pairs={{8,0},{12,4},{9,1},{13,5},{10,2},{14,6},{11,3},{15,7},{24,16},{28,... | collective-permute-start | bytes 393224 | tf_op jit(solution)/shard_map/ppermute | solution.py:15
  17.2 45.7 %collective-permute-start.1 = (f32[4,64,128]{1,2,0:T(8,128)}, f32[4,64,128]{1,2,0:T(8,128)}, u32[]{:S(2)}, u32[]{:S(2)}) collective-permute-start(f32[4,64,128]{1,2,0:T(8,128)} %bitcast.14), channel_id=1, source_target_pairs={{4,0},{8,4},{12,8},{5,1},{9,5},{13,9},{6,2},{10,6},{14,10},{7,3},{... | collective-permute-start | bytes 393224 | tf_op jit(solution)/shard_map/ppermute | solution.py:15
  19.2 43.6 %collective-permute-start.2 = (f32[4,64,128]{1,2,0:T(8,128)}, f32[4,64,128]{1,2,0:T(8,128)}, u32[]{:S(2)}, u32[]{:S(2)}) collective-permute-start(f32[4,64,128]{1,2,0:T(8,128)} %bitcast.16), channel_id=1, source_target_pairs={{0,4},{4,8},{8,12},{1,5},{5,9},{9,13},{2,6},{6,10},{10,14},{3,7},{... | collective-permute-start | bytes 393224 | tf_op jit(solution)/shard_map/ppermute | solution.py:15
  23.7 39.2 %collective-permute-start.3 = (f32[4,64,128]{1,2,0:T(8,128)}, f32[4,64,128]{1,2,0:T(8,128)}, u32[]{:S(2)}, u32[]{:S(2)}) collective-permute-start(f32[4,64,128]{1,2,0:T(8,128)} %bitcast.18), channel_id=1, source_target_pairs={{0,8},{4,12},{1,9},{5,13},{2,10},{6,14},{3,11},{7,15},{16,24},{20,... | collective-permute-start | bytes 393224 | tf_op jit(solution)/shard_map/ppermute | solution.py:15
  34.1 3.9 %copy-start.26 = (s32[32]{0:T(128)S(1)}, s32[32]{0:T(128)}, u32[]{:S(2)}) copy-start(s32[32]{0:T(128)} %fusion.119) | copy-start | bytes 388
  34.1 6.2 %copy-start.13 = (s32[4,4]{1,0:T(4,128)S(1)}, s32[4,4]{1,0:T(4,128)}, u32[]{:S(2)}) copy-start(s32[4,4]{1,0:T(4,128)} %select_reduce_fusion) | copy-start | bytes 196
  34.1 6.9 %copy-start.14 = (f32[1,4,4]{2,1,0:T(4,128)S(1)}, f32[1,4,4]{2,1,0:T(4,128)}, u32[]{:S(2)}) copy-start(f32[1,4,4]{2,1,0:T(4,128)} %get-tuple-element.57) | copy-start | bytes 196
  35.8 5.8 %copy-start.1 = (f32[32,64,64]{2,1,0:T(8,128)S(1)}, f32[32,64,64]{2,1,0:T(8,128)}, u32[]{:S(2)}) copy-start(f32[32,64,64]{2,1,0:T(8,128)} %copy.70) | copy-start | bytes 1572868
  45.1 1.9 copy-start.4
  45.1 1.9 copy-start.6
  45.1 1.9 copy-start.8
  45.2 1.9 copy-start.10
  45.2 1.9 copy-start.28
  47.1 6.3 %copy-start.19 = (pred[4,32]{1,0:T(4,128)(4,1)S(1)}, pred[4,32]{1,0:T(4,128)(4,1)}, u32[]{:S(2)}) copy-start(pred[4,32]{1,0:T(4,128)(4,1)} %copy-done.18) | copy-start | bytes 388
  68.3 11.1 %copy-start.17 = (pred[4,32]{1,0:T(4,128)(4,1)S(1)}, pred[4,32]{1,0:T(4,128)(4,1)}, u32[]{:S(2)}) copy-start(pred[4,32]{1,0:T(4,128)(4,1)} %copy-done.16) | copy-start | bytes 388
  70.2 14.7 %collective-permute-start.4 = (f32[1,64,128]{2,1,0:T(8,128)S(1)}, f32[1,64,128]{2,1,0:T(8,128)S(1)}, u32[]{:S(2)}, u32[]{:S(2)}) collective-permute-start(f32[1,64,128]{2,1,0:T(8,128)S(1)} %get-tuple-element.35), channel_id=1, source_target_pairs={{4,0},{8,4},{12,8},{5,1},{9,5},{13,9},{6,2},{10,6},{14,10},{7,3},{... | collective-permute-start | bytes 98312 | tf_op jit(solution)/shard_map/ppermute | solution.py:28
  71.5 13.4 %collective-permute-start.5 = (f32[1,64,128]{2,1,0:T(8,128)S(1)}, f32[1,64,128]{2,1,0:T(8,128)S(1)}, u32[]{:S(2)}, u32[]{:S(2)}) collective-permute-start(f32[1,64,128]{2,1,0:T(8,128)S(1)} %get-tuple-element.36), channel_id=1, source_target_pairs={{0,4},{4,8},{8,12},{1,5},{5,9},{9,13},{2,6},{6,10},{10,14},{3,7},{... | collective-permute-start | bytes 98312 | tf_op jit(solution)/shard_map/ppermute | solution.py:26
  74.5 9.7 %collective-permute-start.6 = (f32[32,1,128]{2,1,0:T(1,128)S(1)}, f32[32,1,128]{2,1,0:T(1,128)S(1)}, u32[]{:S(2)}, u32[]{:S(2)}) collective-permute-start(f32[32,1,128]{2,1,0:T(1,128)S(1)} %get-tuple-element.37), channel_id=1, source_target_pairs={{1,0},{2,1},{3,2},{0,3},{5,4},{6,5},{7,6},{4,7},{9,8},{10,9},{11,1... | collective-permute-start | bytes 49160 | tf_op jit(solution)/shard_map/ppermute | solution.py:28
  79.3 5.5 %collective-permute-start.7 = (f32[32,1,128]{2,1,0:T(1,128)S(1)}, f32[32,1,128]{2,1,0:T(1,128)S(1)}, u32[]{:S(2)}, u32[]{:S(2)}) collective-permute-start(f32[32,1,128]{2,1,0:T(1,128)S(1)} %get-tuple-element.38), channel_id=1, source_target_pairs={{0,1},{1,2},{2,3},{3,0},{4,5},{5,6},{6,7},{7,4},{8,9},{9,10},{10,1... | collective-permute-start | bytes 49160 | tf_op jit(solution)/shard_map/ppermute | solution.py:26
  82.7 2.1 %copy-start.15 = (f32[32]{0:T(128)S(1)}, f32[32]{0:T(128)}, u32[]{:S(2)}) copy-start(f32[32]{0:T(128)} %param.6) | copy-start | bytes 388
  117.8 1.6 copy-start.2
  118.7 2.6 %copy-start.22 = (f32[16]{0:T(128)S(1)}, f32[16]{0:T(128)}, u32[]{:S(2)}) copy-start(f32[16]{0:T(128)} %get-tuple-element.92) | copy-start | bytes 196
  118.7 2.6 %copy-start.23 = (f32[16]{0:T(128)S(1)}, f32[16]{0:T(128)}, u32[]{:S(2)}) copy-start(f32[16]{0:T(128)} %get-tuple-element.93) | copy-start | bytes 196
  118.7 2.6 %copy-start.24 = (f32[16]{0:T(128)S(1)}, f32[16]{0:T(128)}, u32[]{:S(2)}) copy-start(f32[16]{0:T(128)} %get-tuple-element.94) | copy-start | bytes 196
  118.7 2.6 %copy-start.25 = (f32[16]{0:T(128)S(1)}, f32[16]{0:T(128)}, u32[]{:S(2)}) copy-start(f32[16]{0:T(128)} %get-tuple-element.95) | copy-start | bytes 196
  123.8 13.0 %copy-start = (f32[32,64,64]{2,1,0:T(8,128)S(1)}, f32[32,64,64]{2,1,0:T(8,128)}, u32[]{:S(2)}) copy-start(f32[32,64,64]{2,1,0:T(8,128)} %copy.84) | copy-start | bytes 1572868
  123.9 27.8 %collective-permute-start.8 = (f32[4,64,128]{1,2,0:T(8,128)S(1)}, f32[4,64,128]{1,2,0:T(8,128)S(1)}, u32[]{:S(2)}, u32[]{:S(2)}) collective-permute-start(f32[4,64,128]{1,2,0:T(8,128)S(1)} %bitcast.159), channel_id=1, source_target_pairs={{8,0},{12,4},{9,1},{13,5},{10,2},{14,6},{11,3},{15,7},{24,16},{28,... | collective-permute-start | bytes 393224 | tf_op jit(solution)/shard_map/ppermute | solution.py:15
  125.4 26.4 %collective-permute-start.9 = (f32[4,64,128]{1,2,0:T(8,128)S(1)}, f32[4,64,128]{1,2,0:T(8,128)}, u32[]{:S(2)}, u32[]{:S(2)}) collective-permute-start(f32[4,64,128]{1,2,0:T(8,128)S(1)} %bitcast.160), channel_id=1, source_target_pairs={{4,0},{8,4},{12,8},{5,1},{9,5},{13,9},{6,2},{10,6},{14,10},{7,3},{... | collective-permute-start | bytes 393224 | tf_op jit(solution)/shard_map/ppermute | solution.py:15
  126.7 25.0 %collective-permute-start.10 = (f32[4,64,128]{1,2,0:T(8,128)S(1)}, f32[4,64,128]{1,2,0:T(8,128)}, u32[]{:S(2)}, u32[]{:S(2)}) collective-permute-start(f32[4,64,128]{1,2,0:T(8,128)S(1)} %bitcast.161), channel_id=1, source_target_pairs={{0,4},{4,8},{8,12},{1,5},{5,9},{9,13},{2,6},{6,10},{10,14},{3,7},{... | collective-permute-start | bytes 393224 | tf_op jit(solution)/shard_map/ppermute | solution.py:15
  130.5 9.8 %copy-start.27 = (f32[32]{0:T(128)S(1)}, f32[32]{0:T(128)}, u32[]{:S(2)}) copy-start(f32[32]{0:T(128)} %get-tuple-element.9) | copy-start | bytes 388
  130.5 9.8 %copy-start.29 = (f32[32]{0:T(128)S(1)}, f32[32]{0:T(128)}, u32[]{:S(2)}) copy-start(f32[32]{0:T(128)} %get-tuple-element.83) | copy-start | bytes 388
  130.5 9.8 %copy-start.30 = (f32[32]{0:T(128)S(1)}, f32[32]{0:T(128)}, u32[]{:S(2)}) copy-start(f32[32]{0:T(128)} %get-tuple-element.84) | copy-start | bytes 388
  130.5 9.8 %copy-start.31 = (f32[32]{0:T(128)S(1)}, f32[32]{0:T(128)}, u32[]{:S(2)}) copy-start(f32[32]{0:T(128)} %get-tuple-element.85) | copy-start | bytes 388
  130.5 21.2 %collective-permute-start.11 = (f32[4,64,128]{1,2,0:T(8,128)S(1)}, f32[4,64,128]{1,2,0:T(8,128)}, u32[]{:S(2)}, u32[]{:S(2)}) collective-permute-start(f32[4,64,128]{1,2,0:T(8,128)S(1)} %bitcast.162), channel_id=1, source_target_pairs={{0,8},{4,12},{1,9},{5,13},{2,10},{6,14},{3,11},{7,15},{16,24},{20,... | collective-permute-start | bytes 393224 | tf_op jit(solution)/shard_map/ppermute | solution.py:15
  154.2 10.0 %collective-permute-start.12 = (f32[1,64,128]{2,1,0:T(8,128)S(1)}, f32[1,64,128]{2,1,0:T(8,128)S(1)}, u32[]{:S(2)}, u32[]{:S(2)}) collective-permute-start(f32[1,64,128]{2,1,0:T(8,128)S(1)} %get-tuple-element.27), channel_id=1, source_target_pairs={{4,0},{8,4},{12,8},{5,1},{9,5},{13,9},{6,2},{10,6},{14,10},{7,3},{... | collective-permute-start | bytes 98312 | tf_op jit(solution)/shard_map/ppermute | solution.py:28
  155.5 8.7 %collective-permute-start.13 = (f32[1,64,128]{2,1,0:T(8,128)S(1)}, f32[1,64,128]{2,1,0:T(8,128)S(1)}, u32[]{:S(2)}, u32[]{:S(2)}) collective-permute-start(f32[1,64,128]{2,1,0:T(8,128)S(1)} %get-tuple-element.28), channel_id=1, source_target_pairs={{0,4},{4,8},{8,12},{1,5},{5,9},{9,13},{2,6},{6,10},{10,14},{3,7},{... | collective-permute-start | bytes 98312 | tf_op jit(solution)/shard_map/ppermute | solution.py:26
  158.6 3.8 %collective-permute-start.14 = (f32[32,1,128]{2,1,0:T(1,128)S(1)}, f32[32,1,128]{2,1,0:T(1,128)S(1)}, u32[]{:S(2)}, u32[]{:S(2)}) collective-permute-start(f32[32,1,128]{2,1,0:T(1,128)S(1)} %get-tuple-element.29), channel_id=1, source_target_pairs={{1,0},{2,1},{3,2},{0,3},{5,4},{6,5},{7,6},{4,7},{9,8},{10,9},{11,1... | collective-permute-start | bytes 49160 | tf_op jit(solution)/shard_map/ppermute | solution.py:28
  158.7 5.6 %collective-permute-start.15 = (f32[32,1,128]{2,1,0:T(1,128)S(1)}, f32[32,1,128]{2,1,0:T(1,128)S(1)}, u32[]{:S(2)}, u32[]{:S(2)}) collective-permute-start(f32[32,1,128]{2,1,0:T(1,128)S(1)} %get-tuple-element.30), channel_id=1, source_target_pairs={{0,1},{1,2},{2,3},{3,0},{4,5},{5,6},{6,7},{7,4},{8,9},{9,10},{10,1... | collective-permute-start | bytes 49160 | tf_op jit(solution)/shard_map/ppermute | solution.py:26
where the time goes:
time: 197 us; the launch traced here: 196 us
  blocking collectives  60.2 us (31%)
  starting transfers between devices  40.9 us (21%)
  local copies, waits for them, and re-layouts  39.2 us (20%)
  matrix products  26.7 us (14%)
  other arithmetic  24.1 us (12%)
  waiting for transfers between devices  4.2 us (2%)
    psum x1, blocking collectives, local(): target = lax.psum(column_mass(tracers, weights), ('lat', 'lon'))  30.4 us
    psum x1, blocking collectives, local(): step_total = lax.psum(column_mass(diffused, weights), ('lat', 'lon'))  29.8 us
    ppermute x8, starting transfers between devices, from_behind(): return lax.ppermute(block, axis, route)  25.3 us
    dot_general x4, matrix products, interpolate(): jnp.einsum('nlm,nimt->nilt', weight_z, stacked, precision=lax.Precision.H...  15.1 us
    dot_general x4, matrix products, interpolate(): jnp.einsum('nij,njv->niv', plane_weights, patches, precision=lax.Precisio...  11.6 us
    reshape x2, local copies, waits for them, and re-layouts, interpolate(): return levelled.reshape(patch_count, 64, value_count)  8.25 us
    ppermute x4, starting transfers between devices, extended(): lax.ppermute(tail, axis, [(i, (i + 1) % count) for i in range(ends)])  8.08 us
    transpose x2, local copies, waits for them, and re-layouts, interpolate(): jnp.einsum('nlm,nimt->nilt', weight_z, stacked, precision=lax.Precision.H...  8.02 us
  transfers between devices with their start and end apart: 16, of which 3 were waited for; matrix products, arithmetic and copies ran while one was open for 28% of the time, Pallas kernels for 0%

commit v1 on v0

--- a/solution.py
+++ b/solution.py
@@ -169,7 +169,7 @@
         lat_wide = extended(advected, (("lat", 0),), 1, False)
         laplace = lat_wide[2:] + lat_wide[:-2] + lon_wide[:, 2:] + lon_wide[:, :-2] - 4.0 * advected
         diffused = advected + diffusivity[:, None, None] * laplace
-        step_total = lax.psum(column_mass(diffused, weights), ("lat", "lon"))
+        step_total = lax.psum(lax.psum(column_mass(diffused, weights), "lon"), "lat")
         state_field = diffused * (target / step_total)[None, None, :]
     return state_field
 

time: 197 us -> 199 us (1.010)
    psum x1 -> x4, blocking collectives: 29.8 us -> 31.9 us  [the longest x2 20.4 us: local(): lax.psum(column_mass(diffused, weights), 'lon')]
where the time goes in v1:
time: 199 us; the launch traced here: 198 us
  blocking collectives  61.5 us (31%)
  starting transfers between devices  40.2 us (20%)
  local copies, waits for them, and re-layouts  39.2 us (20%)
  matrix products  26.6 us (13%)
  other arithmetic  24 us (12%)
  waiting for transfers between devices  5.09 us (3%)
    psum x1, blocking collectives, local(): target = lax.psum(column_mass(tracers, weights), ('lat', 'lon'))  29.7 us
    ppermute x8, starting transfers between devices, from_behind(): return lax.ppermute(block, axis, route)  24.3 us
    psum x2, blocking collectives, local(): lax.psum(column_mass(diffused, weights), 'lon')  20.4 us
    dot_general x4, matrix products, interpolate(): jnp.einsum('nlm,nimt->nilt', weight_z, stacked, precision=lax.Precision.H...  15.1 us
    dot_general x4, matrix products, interpolate(): jnp.einsum('nij,njv->niv', plane_weights, patches, precision=lax.Precisio...  11.6 us
    psum x2, blocking collectives, local(): lax.psum(lax.psum(column_mass(diffused, weights), 'lon'), 'lat')  11.5 us
    ppermute x4, starting transfers between devices, extended(): lax.ppermute(head, axis, [((i + 1) % count, i) for i in range(ends)])  8.71 us
    reshape x2, local copies, waits for them, and re-layouts, interpolate(): return levelled.reshape(patch_count, 64, value_count)  8.24 us
  transfers between devices with their start and end apart: 16, of which 3 were waited for; matrix products, arithmetic and copies ran while one was open for 28% of the time, Pallas kernels for 0%

profile of v1, /device:TPU:0, one launch (start us, length us, event | category | flops | bytes accessed | tf_op | source)
XLA Modules:
  0.0 197.6 jit_solution(4569870054052340208)
XLA Ops:
  2.4 1.4 copy.61
  7.4 1.5 copy.62
  9.6 2.9 %fusion.150 = f32[16,64,128]{1,2,0:T(8,128)S(1)} fusion(f32[16,64,64]{2,1,0:T(8,128)} %copy.62, f32[16,64,128]{2,1,0:T(8,128)S(1)} %gather_fusion), kind=kOutput, calls=%fused_computation.360 | convolution fusion | flops 100663296 | bytes 1310720 | tf_op jit(solution)/shard_map/nij,njv->niv/dot_general | solution.py:61
  12.5 2.5 %convolution_bitcast_fusion.1 = f32[16,64,4,32]{1,2,3,0:T(4,128)S(1)} fusion(f32[16,64,4,32]{1,3,2,0:T(8,128)S(1)} %bitcast.153, f32[4,4]{1,0:T(4,128)S(1)} %fusion.111, f32[16]{0:T(128)S(1)} %get-tuple-element.113, f32[4,4]{1,0:T(4,128)S(1)} %fusion.110, f32[16]{0:T(128)S(1)} %get-tuple-element.114, f32[4,4]{1,0:T(4,128)S(1)} %fusion.109, ...), kind=kOutput, calls=%fused_computation.13 | convolution fusion | flops 6293248 | bytes 1049088 | tf_op jit(solution)/shard_map/nlm,nimt->nilt/dot_general | solution.py:66
  15.1 1.3 collective-permute-start
  17.2 1.3 collective-permute-start.1
  19.2 3.7 %collective-permute-start.2 = (f32[4,64,128]{1,2,0:T(8,128)}, f32[4,64,128]{1,2,0:T(8,128)}, u32[]{:S(2)}, u32[]{:S(2)}) collective-permute-start(f32[4,64,128]{1,2,0:T(8,128)} %bitcast.16), channel_id=1, source_target_pairs={{0,4},{4,8},{8,12},{1,5},{5,9},{9,13},{2,6},{6,10},{10,14},{3,7},{... | collective-permute-start | bytes 393224 | tf_op jit(solution)/shard_map/ppermute | solution.py:15
  23.7 6.3 %collective-permute-start.3 = (f32[4,64,128]{1,2,0:T(8,128)}, f32[4,64,128]{1,2,0:T(8,128)}, u32[]{:S(2)}, u32[]{:S(2)}) collective-permute-start(f32[4,64,128]{1,2,0:T(8,128)} %bitcast.18), channel_id=1, source_target_pairs={{0,8},{4,12},{1,9},{5,13},{2,10},{6,14},{3,11},{7,15},{16,24},{20,... | collective-permute-start | bytes 393224 | tf_op jit(solution)/shard_map/ppermute | solution.py:15
  34.0 1.7 copy.70
  37.8 1.2 pad_clamp_fusion
  39.0 1.2 multiply_multiply_fusion.2
  41.6 3.5 %fusion.151 = f32[32,64,128]{1,2,0:T(8,128)S(1)} fusion(f32[32,64,64]{2,1,0:T(8,128)S(1)} %copy-done.1, f32[32,64,128]{2,1,0:T(8,128)S(1)} %gather_fusion.2), kind=kOutput, calls=%fused_computation.361 | convolution fusion | flops 201326592 | bytes 2621440 | tf_op jit(solution)/shard_map/nij,njv->niv/dot_general | solution.py:61
  45.1 1.6 broadcast_multiply_fusion
  47.1 5.5 %fusion.4 = f32[32,64,4,32]{1,2,3,0:T(4,128)} fusion(f32[32,64,4,32]{1,3,2,0:T(8,128)S(1)} %bitcast.143, f32[4,4]{1,0:T(4,128)S(1)} %copy-done.10, f32[32]{0:T(128)S(1)} %get-tuple-element.103, f32[4,4]{1,0:T(4,128)S(1)} %copy-done.8, f32[32]{0:T(128)S(1)} %get-tuple-element.104, f32[4,4]{1,0:T(4,128)S(1)} %copy-done.6, f32[32]{0:T(128)S(1)} %get-tuple-element.102, ...), kind=kOutput, calls=%fused_computation.10 | convolution fusion | flops 12586496 | bytes 2097920 | tf_op jit(solution)/shard_map/nlm,nimt->nilt/dot_general | solution.py:66
  53.3 4.8 %copy.73 = f32[32,64,4,32]{3,2,1,0:T(4,128)} copy(f32[32,64,4,32]{1,2,3,0:T(4,128)} %fusion.4) | data formatting | bytes 2097152 | tf_op jit(solution)/shard_map/nlm,nimt->nilt/transpose | solution.py:66
  58.1 4.5 %reshape.1437 = f32[4,8,8,8,128]{4,3,2,1,0:T(8,128)} reshape(f32[32,64,4,32]{3,2,1,0:T(4,128)} %copy.73) | data formatting | bytes 2097152 | tf_op jit(solution)/shard_map/reshape | solution.py:67
  62.8 2.3 %pad_maximum_fusion.8 = f32[4,4,64,128]{2,3,1,0:T(8,128)} fusion(f32[1,4,64,128]{2,3,1,0:T(8,128)} %bitcast.19, f32[1,4,64,128]{2,3,1,0:T(8,128)} %bitcast.17, f32[1,4,64,128]{2,3,1,0:T(8,128)} %bitcast.15, f32[1,4,64,128]{2,3,1,0:T(8,128)} %bitcast.13), kind=kLoop, calls=%fused_computation.34 | loop fusion | flops 393216 | bytes 1048576 | tf_op jit(solution)/shard_map/stack | solution.py:158
  65.0 1.5 copy.69
  66.6 1.6 gather_fusion.1
  68.2 1.7 select_bitcast_fusion.1
  70.1 1.3 collective-permute-start.4
  71.4 3.0 %collective-permute-start.5 = (f32[1,64,128]{2,1,0:T(8,128)S(1)}, f32[1,64,128]{2,1,0:T(8,128)S(1)}, u32[]{:S(2)}, u32[]{:S(2)}) collective-permute-start(f32[1,64,128]{2,1,0:T(8,128)S(1)} %get-tuple-element.34), channel_id=1, source_target_pairs={{0,4},{4,8},{8,12},{1,5},{5,9},{9,13},{2,6},{6,10},{10,14},{3,7},{... | collective-permute-start | bytes 98312 | tf_op jit(solution)/shard_map/ppermute | solution.py:26
  74.4 4.8 %collective-permute-start.6 = (f32[32,1,128]{2,1,0:T(1,128)S(1)}, f32[32,1,128]{2,1,0:T(1,128)S(1)}, u32[]{:S(2)}, u32[]{:S(2)}) collective-permute-start(f32[32,1,128]{2,1,0:T(1,128)S(1)} %get-tuple-element.35), channel_id=1, source_target_pairs={{1,0},{2,1},{3,2},{0,3},{5,4},{6,5},{7,6},{4,7},{9,8},{10,9},{11,1... | collective-permute-start | bytes 49160 | tf_op jit(solution)/shard_map/ppermute | solution.py:28
  79.3 3.3 %copy.84 = f32[32,64,64]{2,1,0:T(8,128)} copy(f32[32,64,64]{0,2,1:T(8,128)} %bitcast.142) | data formatting | bytes 1048576 | tf_op jit(solution)/shard_map/reshape | solution.py:60
  82.6 1.5 copy.76
  84.8 1.9 multiply_reduce_fusion.1
  86.7 11.9 %psum.36 = f32[128]{0:T(128)S(1)} all-reduce(f32[128]{0:T(128)S(1)} %get-tuple-element.5), channel_id=1, replica_groups=mesh['groups'=2,'lat'=4,'lon'=4] {'lon'}, use_global_device_ids=true, to_apply=%region_10.11 | all-reduce | flops 128 | bytes 1024 | tf_op jit(solution)/shard_map/psum | solution.py:172
  98.5 5.7 %psum.37 = f32[128]{0:T(128)S(1)} all-reduce(f32[128]{0:T(128)S(1)} %psum.36), channel_id=1, replica_groups=mesh['groups'=2,'lat'=4,'lon'=4] {'lat'}, use_global_device_ids=true, to_apply=%region_11.12 | all-reduce | flops 128 | bytes 1024 | tf_op jit(solution)/shard_map/psum | solution.py:172
  104.3 29.7 %psum.35 = f32[128]{0:T(128)S(1)} all-reduce(f32[128]{0:T(128)S(1)} %get-tuple-element.6), channel_id=1, replica_groups=mesh['groups'=2,'lat'=4,'lon'=4] {'lat','lon'}, use_global_device_ids=true, to_apply=%region_8.9 | all-reduce | flops 128 | bytes 1024 | tf_op jit(solution)/shard_map/psum | solution.py:113
  136.2 1.8 fusion.152
  138.1 2.5 %convolution_bitcast_fusion = f32[16,64,4,32]{1,2,3,0:T(4,128)S(1)} fusion(f32[16,64,4,32]{1,3,2,0:T(8,128)S(1)} %bitcast.154, f32[16]{0:T(128)S(1)} %copy-done.24, f32[16]{0:T(128)S(1)} %copy-done.25, f32[16]{0:T(128)S(1)} %copy-done.23, f32[16]{0:T(128)S(1)} %copy-done.22, f32[4,4]{1,0:T(4,128)S(1)} %copy-done.10, f32[4,4]{1,0:T(4,128)S(1)} %copy-done.8, ...), kind=kOutput, calls=%fused_computation.12 | convolution fusion | flops 6293248 | bytes 1049088 | tf_op jit(solution)/shard_map/nlm,nimt->nilt/dot_general | solution.py:66
  140.7 1.4 collective-permute-start.8
  142.2 1.3 collective-permute-start.9
  143.5 3.8 %collective-permute-start.10 = (f32[4,64,128]{1,2,0:T(8,128)S(1)}, f32[4,64,128]{1,2,0:T(8,128)}, u32[]{:S(2)}, u32[]{:S(2)}) collective-permute-start(f32[4,64,128]{1,2,0:T(8,128)S(1)} %bitcast.161), channel_id=1, source_target_pairs={{0,4},{4,8},{8,12},{1,5},{5,9},{9,13},{2,6},{6,10},{10,14},{3,7},{... | collective-permute-start | bytes 393224 | tf_op jit(solution)/shard_map/ppermute | solution.py:15
  147.3 5.3 %collective-permute-start.11 = (f32[4,64,128]{1,2,0:T(8,128)S(1)}, f32[4,64,128]{1,2,0:T(8,128)}, u32[]{:S(2)}, u32[]{:S(2)}) collective-permute-start(f32[4,64,128]{1,2,0:T(8,128)S(1)} %bitcast.162), channel_id=1, source_target_pairs={{0,8},{4,12},{1,9},{5,13},{2,10},{6,14},{3,11},{7,15},{16,24},{20,... | collective-permute-start | bytes 393224 | tf_op jit(solution)/shard_map/ppermute | solution.py:15
  152.6 3.5 %fusion.153 = f32[32,64,128]{1,2,0:T(8,128)S(1)} fusion(f32[32,64,64]{2,1,0:T(8,128)S(1)} %copy-done, f32[32,64,128]{2,1,0:T(8,128)S(1)} %gather_fusion.5), kind=kOutput, calls=%fused_computation.363 | convolution fusion | flops 201326592 | bytes 2621440 | tf_op jit(solution)/shard_map/nij,njv->niv/dot_general | solution.py:61
  156.1 4.5 %fusion.7 = f32[32,64,4,32]{1,2,3,0:T(4,128)S(1)} fusion(f32[32,64,4,32]{1,3,2,0:T(8,128)S(1)} %bitcast.144, f32[32]{0:T(128)S(1)} %copy-done.30, f32[32]{0:T(128)S(1)} %copy-done.31, f32[32]{0:T(128)S(1)} %copy-done.29, f32[32]{0:T(128)S(1)} %copy-done.27, f32[4,4]{1,0:T(4,128)S(1)} %copy-done.10, f32[4,4]{1,0:T(4,128)S(1)} %copy-done.8, ...), kind=kOutput, calls=%fused_computation.11 | convolution fusion | flops 12586496 | bytes 2097920 | tf_op jit(solution)/shard_map/nlm,nimt->nilt/dot_general | solution.py:66
  160.6 3.2 %copy.87 = f32[32,64,4,32]{3,2,1,0:T(4,128)} copy(f32[32,64,4,32]{1,2,3,0:T(4,128)S(1)} %fusion.7) | data formatting | bytes 2097152 | tf_op jit(solution)/shard_map/nlm,nimt->nilt/transpose | solution.py:66
  163.8 3.7 %reshape.1446 = f32[4,8,8,8,128]{4,3,2,1,0:T(8,128)S(1)} reshape(f32[32,64,4,32]{3,2,1,0:T(4,128)} %copy.87) | data formatting | bytes 2097152 | tf_op jit(solution)/shard_map/reshape | solution.py:67
  167.5 1.2 pad_maximum_fusion.9
  170.0 1.3 collective-permute-start.12
  171.3 3.0 %collective-permute-start.13 = (f32[1,64,128]{2,1,0:T(8,128)S(1)}, f32[1,64,128]{2,1,0:T(8,128)S(1)}, u32[]{:S(2)}, u32[]{:S(2)}) collective-permute-start(f32[1,64,128]{2,1,0:T(8,128)S(1)} %get-tuple-element.26), channel_id=1, source_target_pairs={{0,4},{4,8},{8,12},{1,5},{5,9},{9,13},{2,6},{6,10},{10,14},{3,7},{... | collective-permute-start | bytes 98312 | tf_op jit(solution)/shard_map/ppermute | solution.py:26
  174.4 1.3 collective-permute-start.14
  176.7 1.7 collective-permute-done.14
  178.4 2.8 %collective-permute-done.15 = f32[32,1,128]{2,1,0:T(1,128)S(1)} collective-permute-done((f32[32,1,128]{2,1,0:T(1,128)S(1)}, f32[32,1,128]{2,1,0:T(1,128)S(1)}, u32[]{:S(2)}, u32[]{:S(2)}) %collective-permute-start.15) | collective-permute-done | bytes 16416 | tf_op jit(solution)/shard_map/ppermute | solution.py:26
  181.9 8.5 %psum.38 = f32[128]{0:T(128)S(1)} all-reduce(f32[128]{0:T(128)S(1)} %multiply_reduce_fusion), channel_id=1, replica_groups=mesh['groups'=2,'lat'=4,'lon'=4] {'lon'}, use_global_device_ids=true, to_apply=%region_14.15 | all-reduce | flops 128 | bytes 1024 | tf_op jit(solution)/shard_map/psum | solution.py:172
  190.5 5.7 %psum.39 = f32[128]{0:T(128)S(1)} all-reduce(f32[128]{0:T(128)S(1)} %psum.38), channel_id=1, replica_groups=mesh['groups'=2,'lat'=4,'lon'=4] {'lat'}, use_global_device_ids=true, to_apply=%region_15.16 | all-reduce | flops 128 | bytes 1024 | tf_op jit(solution)/shard_map/psum | solution.py:172
  196.2 1.4 broadcast_multiply_fusion.4
  (199 shorter events, 23.6 us)
Async XLA Ops:
  3.8 8.7 %copy-start.3 = (f32[4,4]{1,0:T(4,128)}, f32[4,4]{1,0:T(4,128)S(1)}, u32[]{:S(2)}) copy-start(f32[4,4]{1,0:T(4,128)S(1)} %fusion.108) | copy-start | bytes 196
  3.9 8.6 %copy-start.5 = (f32[4,4]{1,0:T(4,128)}, f32[4,4]{1,0:T(4,128)S(1)}, u32[]{:S(2)}) copy-start(f32[4,4]{1,0:T(4,128)S(1)} %fusion.109) | copy-start | bytes 196
  3.9 8.5 %copy-start.7 = (f32[4,4]{1,0:T(4,128)}, f32[4,4]{1,0:T(4,128)S(1)}, u32[]{:S(2)}) copy-start(f32[4,4]{1,0:T(4,128)S(1)} %fusion.110) | copy-start | bytes 196
  4.0 8.5 %copy-start.9 = (f32[4,4]{1,0:T(4,128)}, f32[4,4]{1,0:T(4,128)S(1)}, u32[]{:S(2)}) copy-start(f32[4,4]{1,0:T(4,128)S(1)} %fusion.111) | copy-start | bytes 196
  4.1 0.6 copy-start.18
  4.1 1.3 copy-start.16
  4.1 1.4 copy-start.12
  4.1 4.8 %copy-start.20 = (pred[4,32]{1,0:T(4,128)(4,1)}, pred[4,32]{1,0:T(4,128)(4,1)S(1)}, u32[]{:S(2)}) copy-start(pred[4,32]{1,0:T(4,128)(4,1)S(1)} %get-tuple-element.127) | copy-start | bytes 388
  5.4 27.4 %copy-start.11 = (s32[4,32]{1,0:T(4,128)}, s32[4,32]{1,0:T(4,128)S(1)}, u32[]{:S(2)}) copy-start(s32[4,32]{1,0:T(4,128)S(1)} %select_reduce_fusion.3) | copy-start | bytes 1540
  15.0 17.7 %copy-start.21 = (pred[4,32]{1,0:T(4,128)(4,1)S(1)}, pred[4,32]{1,0:T(4,128)(4,1)}, u32[]{:S(2)}) copy-start(pred[4,32]{1,0:T(4,128)(4,1)} %copy-done.20) | copy-start | bytes 388
  15.1 47.6 %collective-permute-start = (f32[4,64,128]{1,2,0:T(8,128)S(1)}, f32[4,64,128]{1,2,0:T(8,128)}, u32[]{:S(2)}, u32[]{:S(2)}) collective-permute-start(f32[4,64,128]{1,2,0:T(8,128)S(1)} %bitcast.158), channel_id=1, source_target_pairs={{8,0},{12,4},{9,1},{13,5},{10,2},{14,6},{11,3},{15,7},{24,16},{28,... | collective-permute-start | bytes 393224 | tf_op jit(solution)/shard_map/ppermute | solution.py:15
  17.2 45.6 %collective-permute-start.1 = (f32[4,64,128]{1,2,0:T(8,128)}, f32[4,64,128]{1,2,0:T(8,128)}, u32[]{:S(2)}, u32[]{:S(2)}) collective-permute-start(f32[4,64,128]{1,2,0:T(8,128)} %bitcast.14), channel_id=1, source_target_pairs={{4,0},{8,4},{12,8},{5,1},{9,5},{13,9},{6,2},{10,6},{14,10},{7,3},{... | collective-permute-start | bytes 393224 | tf_op jit(solution)/shard_map/ppermute | solution.py:15
  19.2 43.6 %collective-permute-start.2 = (f32[4,64,128]{1,2,0:T(8,128)}, f32[4,64,128]{1,2,0:T(8,128)}, u32[]{:S(2)}, u32[]{:S(2)}) collective-permute-start(f32[4,64,128]{1,2,0:T(8,128)} %bitcast.16), channel_id=1, source_target_pairs={{0,4},{4,8},{8,12},{1,5},{5,9},{9,13},{2,6},{6,10},{10,14},{3,7},{... | collective-permute-start | bytes 393224 | tf_op jit(solution)/shard_map/ppermute | solution.py:15
  23.7 39.1 %collective-permute-start.3 = (f32[4,64,128]{1,2,0:T(8,128)}, f32[4,64,128]{1,2,0:T(8,128)}, u32[]{:S(2)}, u32[]{:S(2)}) collective-permute-start(f32[4,64,128]{1,2,0:T(8,128)} %bitcast.18), channel_id=1, source_target_pairs={{0,8},{4,12},{1,9},{5,13},{2,10},{6,14},{3,11},{7,15},{16,24},{20,... | collective-permute-start | bytes 393224 | tf_op jit(solution)/shard_map/ppermute | solution.py:15
  34.0 3.8 %copy-start.26 = (s32[32]{0:T(128)S(1)}, s32[32]{0:T(128)}, u32[]{:S(2)}) copy-start(s32[32]{0:T(128)} %fusion.119) | copy-start | bytes 388
  34.0 6.2 %copy-start.13 = (s32[4,4]{1,0:T(4,128)S(1)}, s32[4,4]{1,0:T(4,128)}, u32[]{:S(2)}) copy-start(s32[4,4]{1,0:T(4,128)} %select_reduce_fusion) | copy-start | bytes 196
  34.0 6.9 %copy-start.14 = (f32[1,4,4]{2,1,0:T(4,128)S(1)}, f32[1,4,4]{2,1,0:T(4,128)}, u32[]{:S(2)}) copy-start(f32[1,4,4]{2,1,0:T(4,128)} %get-tuple-element.55) | copy-start | bytes 196
  35.8 5.9 %copy-start.1 = (f32[32,64,64]{2,1,0:T(8,128)S(1)}, f32[32,64,64]{2,1,0:T(8,128)}, u32[]{:S(2)}) copy-start(f32[32,64,64]{2,1,0:T(8,128)} %copy.70) | copy-start | bytes 1572868
  45.1 1.9 copy-start.4
  45.1 1.9 copy-start.6
  45.1 1.9 copy-start.8
  45.1 1.9 copy-start.10
  45.1 1.9 copy-start.28
  47.1 6.2 %copy-start.19 = (pred[4,32]{1,0:T(4,128)(4,1)S(1)}, pred[4,32]{1,0:T(4,128)(4,1)}, u32[]{:S(2)}) copy-start(pred[4,32]{1,0:T(4,128)(4,1)} %copy-done.18) | copy-start | bytes 388
  68.2 11.1 %copy-start.17 = (pred[4,32]{1,0:T(4,128)(4,1)S(1)}, pred[4,32]{1,0:T(4,128)(4,1)}, u32[]{:S(2)}) copy-start(pred[4,32]{1,0:T(4,128)(4,1)} %copy-done.16) | copy-start | bytes 388
  70.1 14.7 %collective-permute-start.4 = (f32[1,64,128]{2,1,0:T(8,128)S(1)}, f32[1,64,128]{2,1,0:T(8,128)S(1)}, u32[]{:S(2)}, u32[]{:S(2)}) collective-permute-start(f32[1,64,128]{2,1,0:T(8,128)S(1)} %get-tuple-element.33), channel_id=1, source_target_pairs={{4,0},{8,4},{12,8},{5,1},{9,5},{13,9},{6,2},{10,6},{14,10},{7,3},{... | collective-permute-start | bytes 98312 | tf_op jit(solution)/shard_map/ppermute | solution.py:28
  71.4 13.4 %collective-permute-start.5 = (f32[1,64,128]{2,1,0:T(8,128)S(1)}, f32[1,64,128]{2,1,0:T(8,128)S(1)}, u32[]{:S(2)}, u32[]{:S(2)}) collective-permute-start(f32[1,64,128]{2,1,0:T(8,128)S(1)} %get-tuple-element.34), channel_id=1, source_target_pairs={{0,4},{4,8},{8,12},{1,5},{5,9},{9,13},{2,6},{6,10},{10,14},{3,7},{... | collective-permute-start | bytes 98312 | tf_op jit(solution)/shard_map/ppermute | solution.py:26
  74.4 9.8 %collective-permute-start.6 = (f32[32,1,128]{2,1,0:T(1,128)S(1)}, f32[32,1,128]{2,1,0:T(1,128)S(1)}, u32[]{:S(2)}, u32[]{:S(2)}) collective-permute-start(f32[32,1,128]{2,1,0:T(1,128)S(1)} %get-tuple-element.35), channel_id=1, source_target_pairs={{1,0},{2,1},{3,2},{0,3},{5,4},{6,5},{7,6},{4,7},{9,8},{10,9},{11,1... | collective-permute-start | bytes 49160 | tf_op jit(solution)/shard_map/ppermute | solution.py:28
  79.2 5.5 %collective-permute-start.7 = (f32[32,1,128]{2,1,0:T(1,128)S(1)}, f32[32,1,128]{2,1,0:T(1,128)S(1)}, u32[]{:S(2)}, u32[]{:S(2)}) collective-permute-start(f32[32,1,128]{2,1,0:T(1,128)S(1)} %get-tuple-element.36), channel_id=1, source_target_pairs={{0,1},{1,2},{2,3},{3,0},{4,5},{5,6},{6,7},{7,4},{8,9},{9,10},{10,1... | collective-permute-start | bytes 49160 | tf_op jit(solution)/shard_map/ppermute | solution.py:26
  82.6 2.1 %copy-start.15 = (f32[32]{0:T(128)S(1)}, f32[32]{0:T(128)}, u32[]{:S(2)}) copy-start(f32[32]{0:T(128)} %param.6) | copy-start | bytes 388
  134.6 1.6 copy-start.2
  135.4 2.6 %copy-start.22 = (f32[16]{0:T(128)S(1)}, f32[16]{0:T(128)}, u32[]{:S(2)}) copy-start(f32[16]{0:T(128)} %get-tuple-element.90) | copy-start | bytes 196
  135.5 2.6 %copy-start.23 = (f32[16]{0:T(128)S(1)}, f32[16]{0:T(128)}, u32[]{:S(2)}) copy-start(f32[16]{0:T(128)} %get-tuple-element.91) | copy-start | bytes 196
  135.5 2.6 %copy-start.24 = (f32[16]{0:T(128)S(1)}, f32[16]{0:T(128)}, u32[]{:S(2)}) copy-start(f32[16]{0:T(128)} %get-tuple-element.92) | copy-start | bytes 196
  135.5 2.6 %copy-start.25 = (f32[16]{0:T(128)S(1)}, f32[16]{0:T(128)}, u32[]{:S(2)}) copy-start(f32[16]{0:T(128)} %get-tuple-element.93) | copy-start | bytes 196
  140.6 12.0 %copy-start = (f32[32,64,64]{2,1,0:T(8,128)S(1)}, f32[32,64,64]{2,1,0:T(8,128)}, u32[]{:S(2)}) copy-start(f32[32,64,64]{2,1,0:T(8,128)} %copy.84) | copy-start | bytes 1572868
  140.7 26.8 %collective-permute-start.8 = (f32[4,64,128]{1,2,0:T(8,128)S(1)}, f32[4,64,128]{1,2,0:T(8,128)S(1)}, u32[]{:S(2)}, u32[]{:S(2)}) collective-permute-start(f32[4,64,128]{1,2,0:T(8,128)S(1)} %bitcast.159), channel_id=1, source_target_pairs={{8,0},{12,4},{9,1},{13,5},{10,2},{14,6},{11,3},{15,7},{24,16},{28,... | collective-permute-start | bytes 393224 | tf_op jit(solution)/shard_map/ppermute | solution.py:15
  142.2 25.3 %collective-permute-start.9 = (f32[4,64,128]{1,2,0:T(8,128)S(1)}, f32[4,64,128]{1,2,0:T(8,128)}, u32[]{:S(2)}, u32[]{:S(2)}) collective-permute-start(f32[4,64,128]{1,2,0:T(8,128)S(1)} %bitcast.160), channel_id=1, source_target_pairs={{4,0},{8,4},{12,8},{5,1},{9,5},{13,9},{6,2},{10,6},{14,10},{7,3},{... | collective-permute-start | bytes 393224 | tf_op jit(solution)/shard_map/ppermute | solution.py:15
  143.5 24.0 %collective-permute-start.10 = (f32[4,64,128]{1,2,0:T(8,128)S(1)}, f32[4,64,128]{1,2,0:T(8,128)}, u32[]{:S(2)}, u32[]{:S(2)}) collective-permute-start(f32[4,64,128]{1,2,0:T(8,128)S(1)} %bitcast.161), channel_id=1, source_target_pairs={{0,4},{4,8},{8,12},{1,5},{5,9},{9,13},{2,6},{6,10},{10,14},{3,7},{... | collective-permute-start | bytes 393224 | tf_op jit(solution)/shard_map/ppermute | solution.py:15
  147.3 8.8 %copy-start.27 = (f32[32]{0:T(128)S(1)}, f32[32]{0:T(128)}, u32[]{:S(2)}) copy-start(f32[32]{0:T(128)} %get-tuple-element.7) | copy-start | bytes 388
  147.3 8.8 %copy-start.29 = (f32[32]{0:T(128)S(1)}, f32[32]{0:T(128)}, u32[]{:S(2)}) copy-start(f32[32]{0:T(128)} %get-tuple-element.81) | copy-start | bytes 388
  147.3 8.8 %copy-start.30 = (f32[32]{0:T(128)S(1)}, f32[32]{0:T(128)}, u32[]{:S(2)}) copy-start(f32[32]{0:T(128)} %get-tuple-element.82) | copy-start | bytes 388
  147.3 8.8 %copy-start.31 = (f32[32]{0:T(128)S(1)}, f32[32]{0:T(128)}, u32[]{:S(2)}) copy-start(f32[32]{0:T(128)} %get-tuple-element.83) | copy-start | bytes 388
  147.3 20.2 %collective-permute-start.11 = (f32[4,64,128]{1,2,0:T(8,128)S(1)}, f32[4,64,128]{1,2,0:T(8,128)}, u32[]{:S(2)}, u32[]{:S(2)}) collective-permute-start(f32[4,64,128]{1,2,0:T(8,128)S(1)} %bitcast.162), channel_id=1, source_target_pairs={{0,8},{4,12},{1,9},{5,13},{2,10},{6,14},{3,11},{7,15},{16,24},{20,... | collective-permute-start | bytes 393224 | tf_op jit(solution)/shard_map/ppermute | solution.py:15
  170.0 11.2 %collective-permute-start.12 = (f32[1,64,128]{2,1,0:T(8,128)S(1)}, f32[1,64,128]{2,1,0:T(8,128)S(1)}, u32[]{:S(2)}, u32[]{:S(2)}) collective-permute-start(f32[1,64,128]{2,1,0:T(8,128)S(1)} %get-tuple-element.25), channel_id=1, source_target_pairs={{4,0},{8,4},{12,8},{5,1},{9,5},{13,9},{6,2},{10,6},{14,10},{7,3},{... | collective-permute-start | bytes 98312 | tf_op jit(solution)/shard_map/ppermute | solution.py:28
  171.3 9.9 %collective-permute-start.13 = (f32[1,64,128]{2,1,0:T(8,128)S(1)}, f32[1,64,128]{2,1,0:T(8,128)S(1)}, u32[]{:S(2)}, u32[]{:S(2)}) collective-permute-start(f32[1,64,128]{2,1,0:T(8,128)S(1)} %get-tuple-element.26), channel_id=1, source_target_pairs={{0,4},{4,8},{8,12},{1,5},{5,9},{9,13},{2,6},{6,10},{10,14},{3,7},{... | collective-permute-start | bytes 98312 | tf_op jit(solution)/shard_map/ppermute | solution.py:26
  174.4 4.0 %collective-permute-start.14 = (f32[32,1,128]{2,1,0:T(1,128)S(1)}, f32[32,1,128]{2,1,0:T(1,128)S(1)}, u32[]{:S(2)}, u32[]{:S(2)}) collective-permute-start(f32[32,1,128]{2,1,0:T(1,128)S(1)} %get-tuple-element.27), channel_id=1, source_target_pairs={{1,0},{2,1},{3,2},{0,3},{5,4},{6,5},{7,6},{4,7},{9,8},{10,9},{11,1... | collective-permute-start | bytes 49160 | tf_op jit(solution)/shard_map/ppermute | solution.py:28
  175.7 5.5 %collective-permute-start.15 = (f32[32,1,128]{2,1,0:T(1,128)S(1)}, f32[32,1,128]{2,1,0:T(1,128)S(1)}, u32[]{:S(2)}, u32[]{:S(2)}) collective-permute-start(f32[32,1,128]{2,1,0:T(1,128)S(1)} %get-tuple-element.28), channel_id=1, source_target_pairs={{0,1},{1,2},{2,3},{3,0},{4,5},{5,6},{6,7},{7,4},{8,9},{9,10},{10,1... | collective-permute-start | bytes 49160 | tf_op jit(solution)/shard_map/ppermute | solution.py:26
